TPU v7x, 128 devices: a whole 4x4x4 slice. The times are simulated.
128 devices in a mesh: row: 4 (over x), col: 32 (over z, y, core).
Axes of the slice: x: 4, y: 4, z: 4, core: 2. Of those that a mesh axis runs over, the one named last changes fastest.
Arguments:
- child_factors: bfloat16 [2, 2048, 8192], P(None, 'col', 'row'), may hold values from -0.0625 to 0.0625
- child_tiles: int32 [2, 16], replicated, may hold values from 0 to 63, as said below
- root_diag: float32 [8192], P('col'), may hold values from 0.5 to 4
Outputs:
- front_out: float32 [8192, 8192], P('row', 'col')
Inputs may be any that keep to these rules, and one draw needn't show every extreme that they name: `child_tiles`: each row lists 2048 / 128 distinct root tiles in increasing order; the first child's list holds tile 0 and the second child's holds the last tile. For every r below 4, exactly 2048 / (128 * 4) tiles t of each row have ((t * 128) // 256) % 4 == r.
All inputs are finite; a program needn't handle non-finite values.
Results may differ from a plain program's by a relative error of at most 0.0003.
Values may be sent and summed in bfloat16 or wider, within the bound.
No kernel may reach another device: no remote copies, remote signals or barrier semaphores. Data moves between devices by JAX's collectives and lax.ppermute only.
A program may use at most 128 MiB of HBM per device.

v0:
```python
import jax
import jax.numpy as jnp
from jax import lax
from jax.sharding import PartitionSpec as P

TILE = 128
NPAN = 1


def pick_tiles(tiles4, index):
    return jnp.take_along_axis(tiles4, index[:, :, None, None], axis=1)


def shards(child_factors, child_tiles, root_diag):
    highest = lax.Precision.HIGHEST
    row_count = lax.axis_size("row")
    block_size = root_diag.shape[0]
    col_count = lax.axis_size("col")
    order_total = block_size * col_count
    loc_rows = order_total // row_count
    row_index = lax.axis_index("row")
    col_index = lax.axis_index("col")
    n_child = child_tiles.shape[0]
    tiles_child = child_tiles.shape[1]
    per_group = tiles_child // row_count
    tiles_block = block_size // TILE
    loc_tiles = loc_rows // TILE
    gathered = lax.all_gather(child_factors, "col", axis=1, tiled=True)
    k_loc = gathered.shape[2]
    tiles4 = gathered.reshape(n_child, tiles_child, TILE, k_loc)
    full_diag = lax.all_gather(root_diag, "col", axis=0, tiled=True)
    owner = child_tiles * TILE // block_size % row_count
    position = jnp.arange(tiles_child, dtype=jnp.int32)
    key = owner * tiles_child + position[None, :]
    rank = jnp.sum(key[:, None, :] < key[:, :, None], axis=2).astype(jnp.int32)
    order = jnp.sum(
        jnp.where(rank[:, :, None] == position[None, None, :], position[None, :, None], 0), axis=1
    ).astype(jnp.int32)
    grouped = pick_tiles(tiles4, order)
    own_tiles = col_index * tiles_block + jnp.arange(tiles_block, dtype=jnp.int32)
    pivot_tiles = jnp.arange(NPAN * tiles_block, dtype=jnp.int32)
    wanted = jnp.concatenate([own_tiles, pivot_tiles])
    match = child_tiles[:, :, None] == wanted[None, None, :]
    where_at = jnp.sum(jnp.where(match, position[None, :, None], 0), axis=1).astype(jnp.int32)
    present = jnp.any(match, axis=1)
    col_rows = pick_tiles(tiles4, where_at)
    col_rows = jnp.where(present[:, :, None, None], col_rows, jnp.zeros_like(col_rows))
    n_cols = wanted.shape[0] * TILE
    col_rows = col_rows.reshape(n_child, n_cols, k_loc)
    pivot_rows = col_rows[:, tiles_block * TILE :]
    grouped = grouped.reshape(n_child, row_count, per_group * TILE, k_loc)
    main = jnp.einsum("cgnk,cmk->gcnm", grouped, col_rows, preferred_element_type=jnp.float32)
    extra = jnp.einsum("cnk,cmk->cnm", pivot_rows, col_rows, preferred_element_type=jnp.float32)
    extra = jnp.broadcast_to(extra[None], (row_count,) + extra.shape)
    packed = jnp.concatenate([main, extra], axis=2)
    chunk_rows = packed.shape[2]
    reduced = lax.psum_scatter(
        packed.reshape(row_count * n_child * chunk_rows, n_cols),
        "row",
        scatter_dimension=0,
        tiled=True,
    ).reshape(n_child, chunk_rows, n_cols)
    mine = reduced[:, : per_group * TILE]
    pivot_part = jnp.sum(reduced[:, per_group * TILE :], axis=0)
    own_w = tiles_block * TILE
    lead_rows = NPAN * block_size
    pivot_diag = full_diag[:lead_rows]
    front00 = pivot_part[:, own_w:] + jnp.diag(pivot_diag)
    lead = jnp.tril(jnp.linalg.cholesky(front00))
    inv_t = lax.linalg.triangular_solve(
        lead, jnp.eye(lead_rows, dtype=jnp.float32), left_side=False, lower=True, transpose_a=True
    )
    cols_panel = jnp.where(col_index == 0, front00, pivot_part[:, :own_w]).T
    my_tiles = lax.dynamic_slice_in_dim(order, row_index * per_group, per_group, axis=1)
    my_root = jnp.take_along_axis(child_tiles, my_tiles, axis=1)
    my_local = my_root * TILE // block_size // row_count * tiles_block + my_root % tiles_block
    loc_index = jnp.arange(loc_tiles, dtype=jnp.int32)
    hit = my_local[:, None, :] == loc_index[None, :, None]
    src = jnp.sum(jnp.where(hit, jnp.arange(per_group, dtype=jnp.int32)[None, None, :], 0), axis=2)
    got = jnp.any(hit, axis=2)
    mine4 = mine.reshape(n_child, per_group, TILE, n_cols)
    placed = pick_tiles(mine4, src.astype(jnp.int32))
    placed = jnp.where(got[:, :, None, None], placed, jnp.zeros_like(placed))
    front_loc = jnp.sum(placed, axis=0).reshape(loc_rows, n_cols)
    local_rows = jnp.arange(loc_rows, dtype=jnp.int32)
    row_block = row_index + local_rows // block_size * row_count
    glob_rows = row_block * block_size + local_rows % block_size
    glob_cols = col_index * block_size + jnp.arange(block_size, dtype=jnp.int32)
    diag_own = jnp.where(glob_rows[:, None] == glob_cols[None, :], root_diag[None, :], 0.0)
    diag_pivot = jnp.where(
        glob_rows[:, None] == jnp.arange(lead_rows, dtype=jnp.int32)[None, :],
        pivot_diag[None, :],
        0.0,
    )
    front_own = front_loc[:, :own_w] + diag_own
    front_pivot = front_loc[:, own_w:] + diag_pivot
    below_rows = jnp.dot(front_pivot, inv_t, precision=highest)
    below_cols = jnp.dot(cols_panel, inv_t, precision=highest)
    schur = front_own - jnp.dot(below_rows, below_cols.T, precision=highest)
    in_lead = (row_block < NPAN)[:, None]
    lead_tiled = jnp.tile(lead, (loc_rows // lead_rows, 1))
    first_col = jnp.where(in_lead, lead_tiled, below_rows)
    rest = jnp.where(in_lead, 0.0, schur)
    return jnp.where(col_index < NPAN, first_col, rest)


def solution(mesh):
    placed = (P(None, "col", "row"), P(), P("col"))
    return jax.shard_map(
        shards, mesh=mesh, in_specs=placed, out_specs=P("row", "col"), check_vma=False
    )
```

profile of v0, /device:TPU:1, one launch (start us, length us, event | category | flops | bytes accessed | tf_op | source)
XLA Modules:
  0.0 355.4 jit_solution(1006790094316008561)
XLA Ops:
  6.5 0.7 all-gather.3.cloned.1.call-update
  7.4 0.9 fusion.44
  8.4 0.7 fusion.48
  9.5 0.9 compare_reduce_fusion
  10.6 75.4 %all-gather.3.cloned.1.call-done = bf16[2,2048,2048]{2,1,0:T(8,128)(2,1)} async-done(((bf16[2,64,2048]{2,1,0:T(8,128)(2,1)}), bf16[2,2048,2048]{2,1,0:T(8,128)(2,1)}) %all-gather.3.cloned.1.call-update) | async-done | bytes 16777232 | tf_op jit(solution)/shard_map/all_gather | solution.py:28
  86.0 8.6 %gather_fusion = bf16[8,128,2048]{2,1,0:T(8,128)(2,1)} fusion(bf16[2,16,128,2048]{3,2,1,0:T(8,128)(2,1)} %bitcast.84, s32[8]{0:T(128)S(1)} %reshape.246), kind=kCustom, calls=%fused_computation | custom fusion | bytes 8388672 | tf_op jit(solution)/shard_map/jit(take_along_axis)/gather | solution.py:11
  94.6 13.1 %gather_fusion.1 = bf16[32,128,2048]{2,1,0:T(8,128)(2,1)} fusion(bf16[2,16,128,2048]{3,2,1,0:T(8,128)(2,1)} %bitcast.85, s32[32]{0:T(128)S(1)} %reshape.252), kind=kCustom, calls=%fused_computation.1 | custom fusion | bytes 33554688 | tf_op jit(solution)/shard_map/jit(take_along_axis)/gather | solution.py:11
  107.7 2.6 fusion.5
  110.3 1.9 copy-done.1
  112.2 1.3 fusion.14
  113.5 15.7 %fusion.6 = f32[4,2,512,512]{3,2,0,1:T(8,128)} fusion(bf16[2,4,512,2048]{3,2,1,0:T(8,128)(2,1)} %bitcast.88, pred[2,4,512]{2,1,0:T(4,128)(4,1)S(1)} %broadcast_in_dim.194, bf16[2,512,2048]{2,1,0:T(8,128)(2,1)} %copy-done.1), kind=kOutput, calls=%fused_computation.15 | convolution fusion | flops 8598323200 | bytes 29364224 | tf_op jit(solution)/shard_map/cgnk,cmk->gcnm/dot_general | solution.py:52
  129.2 0.5 broadcast_in_dim.197
  129.8 8.4 %pad_maximum_fusion = f32[4,2,768,512]{3,2,0,1:T(8,128)} fusion(f32[4,2,256,512]{3,2,0,1:T(8,128)S(1)} %broadcast_in_dim.197, f32[4,2,512,512]{3,2,0,1:T(8,128)} %fusion.6), kind=kLoop, calls=%fused_computation.9 | loop fusion | flops 3145728 | bytes 25165824 | tf_op jit(solution)/shard_map/concatenate | solution.py:55
  138.2 10.7 %copy.27 = f32[4,2,768,512]{3,2,1,0:T(8,128)} copy(f32[4,2,768,512]{3,2,0,1:T(8,128)} %pad_maximum_fusion) | data formatting | bytes 25165824 | tf_op jit(solution)/shard_map/concatenate | solution.py:55
  148.9 0.6 copy-done.5
  149.5 24.2 %all-gather = f32[32,1,256]{2,1,0:T(1,128)S(1)} all-gather(f32[1,1,256]{2,1,0:T(1,128)S(1)} %bitcast.95), channel_id=1, replica_groups=mesh['row'=4,'col'=32] {'col'}, dimensions={0}, use_global_device_ids=true | all-gather | bytes 33792 | tf_op jit(solution)/shard_map/all_gather | solution.py:31
  173.9 0.7 gather_fusion.2
  174.9 0.6 iota_multiply_fusion
  175.5 0.6 iota_add_fusion
  176.1 0.6 fusion.45
  176.7 0.5 compare_and_fusion
  177.2 85.2 %reduce-scatter.2.cloned.1.call-done = f32[1536,512]{1,0:T(8,128)} async-done(((f32[6144,512]{1,0:T(8,128)}), f32[1536,512]{1,0:T(8,128)}) %reduce-scatter.2.cloned.1.call-update) | async-done | bytes 3145744 | tf_op jit(solution)/shard_map/reduce_scatter | solution.py:57
  262.4 1.4 slice_reduce_fusion
  264.2 11.7 %cholesky.49 = f32[128,128]{1,0:T(8,128)S(1)} custom-call(f32[128,128]{1,0:T(8,128)S(1)} %cholesky.115), custom_call_target="Cholesky" | custom-call | tf_op jit(solution)/shard_map/jit(cholesky)/cholesky | solution.py:69
  275.9 9.8 %custom-call.14 = f32[1,128,128]{1,2,0:T(8,128)S(1)} custom-call(f32[1,128,128]{2,1,0:T(8,128)S(1)} %get-tuple-element.44), custom_call_target="InvertDiagBlocksLowerTriangular" | custom-call | tf_op jit(solution)/shard_map/jit(cholesky)/cholesky | solution.py:69
  285.7 0.2 fusion.29
  286.0 0.3 convolution_subtract_fusion.2
  286.2 11.7 %cholesky.103 = f32[128,128]{1,0:T(8,128)S(1)} custom-call(f32[128,128]{1,0:T(8,128)S(1)} %convolution_subtract_fusion.2), custom_call_target="Cholesky" | custom-call | tf_op jit(solution)/shard_map/jit(cholesky)/cholesky | solution.py:69
  298.3 1.8 slice.99
  300.1 0.7 compare_reduce_fusion.1
  300.8 0.6 compare_reduce_fusion.2
  302.8 0.7 triangular_solve.45
  303.6 4.3 %while.1 = (s32[]{:T(128)}, f32[256,256]{0,1:T(8,128)S(1)}, s32[2,2]{1,0:T(2,128)S(1)}, f32[2,128,128]{2,1,0:T(8,128)S(1)}, s32[]{:T(128)}) while((s32[]{:T(128)}, f32[256,256]{0,1:T(8,128)S(1)}, s32[2,2]{1,0:T(2,128)S(1)}, f32[2,128,128]{2,1,0:T(8,128)S(1)}, s32[]{:T(128)}) %tuple.28), condition=%wide.while_cond, body=%wide.while_body.sunk | while | flops 2 | bytes 393321 | solution.py:70
  303.6 0.6 fusion.74
  304.2 1.4 dynamic-slice.7
  305.8 0.6 fusion.74
  306.4 1.4 dynamic-slice.7
  307.9 0.6 copy-done.10
  308.6 20.5 %custom-call.15 = f32[2,128,128]{1,2,0:T(8,128)S(1)} custom-call(f32[2,128,128]{2,1,0:T(8,128)} %copy-done.10), custom_call_target="InvertDiagBlocksLowerTriangular" | custom-call | tf_op jit(solution)/shard_map/triangular_solve | solution.py:70
  329.1 0.6 copy-done.2
  329.7 0.3 fusion.24
  330.0 0.3 convolution_subtract_fusion.1
  330.3 1.2 fusion.27
  331.8 4.3 %gather_fusion.3 = f32[32,128,512]{2,1,0:T(8,128)} fusion(f32[2,4,128,512]{3,2,1,0:T(8,128)S(1)} %bitcast.81, s32[32]{0:T(128)S(1)} %reshape.264), kind=kCustom, calls=%fused_computation.3 | custom fusion | bytes 16777472 | tf_op jit(solution)/shard_map/jit(take_along_axis)/gather | solution.py:11
  336.1 0.4 fusion.21
  336.5 6.1 %select_reduce_fusion = f32[16,128,512]{2,1,0:T(8,128)S(1)} fusion(f32[2,16,128,512]{3,2,1,0:T(8,128)} %bitcast.83, pred[2,16]{1,0:T(4,128)(4,1)S(1)} %copy-done.9, pred[2,16]{1,0:T(4,128)(4,1)S(1)} %copy-done.8), kind=kLoop, calls=%fused_computation.10 | loop fusion | flops 5242880 | bytes 12582976 | tf_op jit(solution)/shard_map/reduce_sum | solution.py:84
  342.6 2.0 bitcast_select_fusion.1
  344.7 3.9 %fusion.12 = f32[2048,256]{1,0:T(8,128)} fusion(f32[2048,256]{1,0:T(8,128)S(1)} %get-tuple-element.45, f32[2048,256]{1,0:T(8,128)S(1)} %get-tuple-element.46, f32[256,256]{1,0:T(8,128)S(1)} %fusion.21, f32[2048,512]{1,0:T(8,128)S(1)} %bitcast.87, f32[256]{0:T(256)S(1)} %copy-done.6, s32[256]{0:T(256)S(1)} %copy-done.7, s32[2048]{0:T(1024)S(1)} %fusion.40, ...), kind=kOutput, calls=%fused_computation.18 | convolution fusion | flops 1613758464 | bytes 8663041 | tf_op jit(solution)/shard_map/dot_general | solution.py:99
  (72 shorter events, 2.7 us)
Async XLA Ops:
  6.5 79.4 %all-gather.3.cloned.1.call-start = ((), (), s32[]{:S(2)}) async-start(), calls=%async_computation.1 | async-start | bytes 17301504 | tf_op jit(solution)/shard_map/all_gather | solution.py:28
  7.3 255.1 %reduce-scatter.2.cloned.1.call-start = ((), (), s32[]{:S(2)}) async-start(), calls=%async_computation.2 | async-start | bytes 15728640 | tf_op jit(solution)/shard_map/reduce_scatter | solution.py:57
  110.3 1.9 copy-start.1
  148.8 0.7 copy-start.5
  148.8 25.0 %copy-start = (s32[2,16]{1,0:T(2,128)S(1)}, s32[2,16]{1,0:T(2,128)}, u32[]{:S(2)}) copy-start(s32[2,16]{1,0:T(2,128)} %param.4) | copy-start | bytes 388
  173.7 90.4 %copy-start.3 = (f32[1,1,256]{2,1,0:T(1,128)}, f32[1,1,256]{2,1,0:T(1,128)S(1)}, u32[]{:S(2)}) copy-start(f32[1,1,256]{2,1,0:T(1,128)S(1)} %slice.98) | copy-start | bytes 3076
  307.9 0.7 copy-start.10
  329.1 0.7 copy-start.2
  331.8 4.8 %copy-start.8 = (pred[2,16]{1,0:T(4,128)(4,1)S(1)}, pred[2,16]{1,0:T(4,128)(4,1)}, u32[]{:S(2)}) copy-start(pred[2,16]{1,0:T(4,128)(4,1)} %fusion.45) | copy-start | bytes 100
  331.8 4.8 %copy-start.9 = (pred[2,16]{1,0:T(4,128)(4,1)S(1)}, pred[2,16]{1,0:T(4,128)(4,1)}, u32[]{:S(2)}) copy-start(pred[2,16]{1,0:T(4,128)(4,1)} %compare_and_fusion) | copy-start | bytes 100
  336.5 6.1 %copy-start.4 = (f32[1,1,256]{2,1,0:T(1,128)S(1)}, f32[1,1,256]{2,1,0:T(1,128)}, u32[]{:S(2)}) copy-start(f32[1,1,256]{2,1,0:T(1,128)} %copy-done.3) | copy-start | bytes 3076
  342.6 2.1 copy-start.6
  342.6 2.1 copy-start.7
Sparse Core Ops, SparseCore 0:
  9.6 76.2 all-gather.2
  149.0 113.3 reduce-scatter.1
where the time goes:
time: 356 us; the launch traced here: 355 us
  waiting for transfers between devices  161 us (45%)
  other arithmetic  79 us (22%)
  local copies, waits for them, and re-layouts  50.1 us (14%)
  matrix products  25.5 us (7%)
  blocking collectives  24.2 us (7%)
  between operations  15.2 us (4%)
    reduce_scatter x1, waiting for transfers between devices, shards(): lax.psum_scatter(packed.reshape(row_count * n_child * chunk_rows, n_cols)...  85.2 us
    all_gather x1, waiting for transfers between devices, shards(): gathered = lax.all_gather(child_factors, 'col', axis=1, tiled=True)  75.4 us
    another operation x7, other arithmetic, shards(): lead = jnp.tril(jnp.linalg.cholesky(front00))  34.7 us
    gather x6, local copies, waits for them, and re-layouts, pick_tiles(): return jnp.take_along_axis(tiles4, index[:, :, None, None], axis=1)  26.3 us
    all_gather x1, blocking collectives, shards(): full_diag = lax.all_gather(root_diag, 'col', axis=0, tiled=True)  24.2 us
    another operation x3, other arithmetic, shards(): lax.linalg.triangular_solve(lead, jnp.eye(lead_rows, dtype=jnp.float32),...  21.1 us
    dot_general x1, matrix products, shards(): jnp.einsum('cgnk,cmk->gcnm', grouped, col_rows, preferred_element_type=jn...  15.7 us
    concatenate x1, local copies, waits for them, and re-layouts, shards(): packed = jnp.concatenate([main, extra], axis=2)  10.7 us
  transfers between devices with their start and end apart: 2, of which 2 were waited for; matrix products, arithmetic and copies ran while one was open for 2% of the time, Pallas kernels for 0%

commit v1 on v0

--- a/solution.py
+++ b/solution.py
@@ -28,7 +28,15 @@
     gathered = lax.all_gather(child_factors, "col", axis=1, tiled=True)
     k_loc = gathered.shape[2]
     tiles4 = gathered.reshape(n_child, tiles_child, TILE, k_loc)
-    full_diag = lax.all_gather(root_diag, "col", axis=0, tiled=True)
+    full_diag = jnp.concatenate(
+        lax.all_to_all(
+            jnp.stack([root_diag for _ in range(lax.axis_size("col"))]),
+            axis_name="col",
+            split_axis=0,
+            concat_axis=0,
+        ),
+        axis=0,
+    )
     owner = child_tiles * TILE // block_size % row_count
     position = jnp.arange(tiles_child, dtype=jnp.int32)
     key = owner * tiles_child + position[None, :]

time: 356 us -> 356 us (level)
  blocking collectives: 24.2 us -> 0 us
  waiting for transfers between devices: 161 us -> 180 us
  starting transfers between devices: 0.04 us -> 5.48 us
    all_gather x1 -> x0, blocking collectives: 24.2 us -> none  [shards(): full_diag = lax.all_gather(root_diag, 'col', axis=0, tiled=True)]
    reduce_scatter x1, waiting for transfers between devices: 85.2 us -> 99.6 us  [shards(): lax.psum_scatter(packed.reshape(row_count * n_child * chunk_rows, n_cols)...]
    all_to_all x0 -> x1, starting transfers between devices: none -> 5.43 us  [shards(): lax.all_to_all(jnp.stack([root_diag for _ in range(lax.axis_size('col'))]...]
    all_to_all x0 -> x1, waiting for transfers between devices: none -> 3.79 us  [shards(): lax.all_to_all(jnp.stack([root_diag for _ in range(lax.axis_size('col'))]...]
  transfers between devices with their start and end apart: 2 -> 3, of which waited for: 2 -> 3; matrix products, arithmetic and copies ran while one was open for 2% -> 2% of each run, Pallas kernels for 0% -> 0%
where the time goes in v1:
time: 356 us; the launch traced here: 355 us
  waiting for transfers between devices  180 us (51%)
  other arithmetic  79 us (22%)
  local copies, waits for them, and re-layouts  50.7 us (14%)
  matrix products  25.5 us (7%)
  between operations  15.1 us (4%)
  starting transfers between devices  5.48 us (2%)
    reduce_scatter x1, waiting for transfers between devices, shards(): lax.psum_scatter(packed.reshape(row_count * n_child * chunk_rows, n_cols)...  99.6 us
    all_gather x1, waiting for transfers between devices, shards(): gathered = lax.all_gather(child_factors, 'col', axis=1, tiled=True)  75.4 us
    another operation x7, other arithmetic, shards(): lead = jnp.tril(jnp.linalg.cholesky(front00))  34.7 us
    gather x6, local copies, waits for them, and re-layouts, pick_tiles(): return jnp.take_along_axis(tiles4, index[:, :, None, None], axis=1)  26.3 us
    another operation x3, other arithmetic, shards(): lax.linalg.triangular_solve(lead, jnp.eye(lead_rows, dtype=jnp.float32),...  21.1 us
    dot_general x1, matrix products, shards(): jnp.einsum('cgnk,cmk->gcnm', grouped, col_rows, preferred_element_type=jn...  15.7 us
    concatenate x1, local copies, waits for them, and re-layouts, shards(): packed = jnp.concatenate([main, extra], axis=2)  10.7 us
    concatenate x1, other arithmetic, shards(): packed = jnp.concatenate([main, extra], axis=2)  8.39 us
  transfers between devices with their start and end apart: 3, of which 3 were waited for; matrix products, arithmetic and copies ran while one was open for 2% of the time, Pallas kernels for 0%

profile of v1, /device:TPU:1, one launch (start us, length us, event | category | flops | bytes accessed | tf_op | source)
XLA Modules:
  0.0 355.4 jit_solution(241768801237081870)
XLA Ops:
  6.5 0.7 all-gather.2.cloned.1.call-update
  7.4 0.9 fusion.44
  8.4 0.7 fusion.48
  9.5 0.9 compare_reduce_fusion
  10.6 75.4 %all-gather.2.cloned.1.call-done = bf16[2,2048,2048]{2,1,0:T(8,128)(2,1)} async-done(((bf16[2,64,2048]{2,1,0:T(8,128)(2,1)}), bf16[2,2048,2048]{2,1,0:T(8,128)(2,1)}) %all-gather.2.cloned.1.call-update) | async-done | bytes 16777232 | tf_op jit(solution)/shard_map/all_gather | solution.py:28
  86.0 8.6 %gather_fusion = bf16[8,128,2048]{2,1,0:T(8,128)(2,1)} fusion(bf16[2,16,128,2048]{3,2,1,0:T(8,128)(2,1)} %bitcast.83, s32[8]{0:T(128)S(1)} %reshape.259), kind=kCustom, calls=%fused_computation | custom fusion | bytes 8388672 | tf_op jit(solution)/shard_map/jit(take_along_axis)/gather | solution.py:11
  94.6 13.1 %gather_fusion.1 = bf16[32,128,2048]{2,1,0:T(8,128)(2,1)} fusion(bf16[2,16,128,2048]{3,2,1,0:T(8,128)(2,1)} %bitcast.84, s32[32]{0:T(128)S(1)} %reshape.265), kind=kCustom, calls=%fused_computation.1 | custom fusion | bytes 33554688 | tf_op jit(solution)/shard_map/jit(take_along_axis)/gather | solution.py:11
  107.7 2.6 fusion.5
  110.3 1.9 copy-done.1
  112.2 1.3 fusion.14
  113.5 15.7 %fusion.6 = f32[4,2,512,512]{3,2,0,1:T(8,128)} fusion(bf16[2,4,512,2048]{3,2,1,0:T(8,128)(2,1)} %bitcast.87, pred[2,4,512]{2,1,0:T(4,128)(4,1)S(1)} %broadcast_in_dim.196, bf16[2,512,2048]{2,1,0:T(8,128)(2,1)} %copy-done.1), kind=kOutput, calls=%fused_computation.15 | convolution fusion | flops 8598323200 | bytes 29364224 | tf_op jit(solution)/shard_map/cgnk,cmk->gcnm/dot_general | solution.py:60
  129.2 0.5 broadcast_in_dim.199
  129.8 8.4 %pad_maximum_fusion = f32[4,2,768,512]{3,2,0,1:T(8,128)} fusion(f32[4,2,256,512]{3,2,0,1:T(8,128)S(1)} %broadcast_in_dim.199, f32[4,2,512,512]{3,2,0,1:T(8,128)} %fusion.6), kind=kLoop, calls=%fused_computation.9 | loop fusion | flops 3145728 | bytes 25165824 | tf_op jit(solution)/shard_map/concatenate | solution.py:63
  138.2 10.7 %copy.27 = f32[4,2,768,512]{3,2,1,0:T(8,128)} copy(f32[4,2,768,512]{3,2,0,1:T(8,128)} %pad_maximum_fusion) | data formatting | bytes 25165824 | tf_op jit(solution)/shard_map/concatenate | solution.py:63
  148.8 0.7 copy-done.5
  149.5 0.6 stack.2
  150.1 5.4 %all-to-all-start = ((f32[32,1,256]{2,1,0:T(1,128)}), f32[32,1,256]{2,1,0:T(1,128)S(1)}, u32[]{:S(2)}, u32[]{:S(2)}) async-start(f32[32,1,256]{2,1,0:T(1,128)} %stack.2), calls=%async_computation.1 | async-start | bytes 65536 | tf_op jit(solution)/shard_map/all_to_all | solution.py:32
  155.7 0.7 gather_fusion.2
  156.5 0.5 iota_add_fusion
  157.2 0.6 fusion.45
  157.9 0.5 compare_and_fusion
  158.4 0.6 iota_multiply_fusion
  159.0 3.8 %all-to-all-done = f32[32,1,256]{2,1,0:T(1,128)S(1)} async-done(((f32[32,1,256]{2,1,0:T(1,128)}), f32[32,1,256]{2,1,0:T(1,128)S(1)}, u32[]{:S(2)}, u32[]{:S(2)}) %all-to-all-start) | async-done | bytes 32800 | tf_op jit(solution)/shard_map/all_to_all | solution.py:32
  162.8 99.6 %reduce-scatter.2.cloned.1.call-done = f32[1536,512]{1,0:T(8,128)} async-done(((f32[6144,512]{1,0:T(8,128)}), f32[1536,512]{1,0:T(8,128)}) %reduce-scatter.2.cloned.1.call-update) | async-done | bytes 3145744 | tf_op jit(solution)/shard_map/reduce_scatter | solution.py:65
  262.5 1.4 slice_reduce_fusion
  264.2 11.7 %cholesky.49 = f32[128,128]{1,0:T(8,128)S(1)} custom-call(f32[128,128]{1,0:T(8,128)S(1)} %cholesky.115), custom_call_target="Cholesky" | custom-call | tf_op jit(solution)/shard_map/jit(cholesky)/cholesky | solution.py:77
  276.0 9.8 %custom-call.14 = f32[1,128,128]{1,2,0:T(8,128)S(1)} custom-call(f32[1,128,128]{2,1,0:T(8,128)S(1)} %get-tuple-element.44), custom_call_target="InvertDiagBlocksLowerTriangular" | custom-call | tf_op jit(solution)/shard_map/jit(cholesky)/cholesky | solution.py:77
  286.0 0.3 convolution_subtract_fusion.2
  286.3 11.7 %cholesky.103 = f32[128,128]{1,0:T(8,128)S(1)} custom-call(f32[128,128]{1,0:T(8,128)S(1)} %convolution_subtract_fusion.2), custom_call_target="Cholesky" | custom-call | tf_op jit(solution)/shard_map/jit(cholesky)/cholesky | solution.py:77
  298.3 1.8 slice.100
  300.1 0.7 compare_reduce_fusion.1
  300.8 0.6 compare_reduce_fusion.2
  302.9 0.7 triangular_solve.45
  303.6 4.3 %while.1 = (s32[]{:T(128)}, f32[256,256]{0,1:T(8,128)S(1)}, s32[2,2]{1,0:T(2,128)S(1)}, f32[2,128,128]{2,1,0:T(8,128)S(1)}, s32[]{:T(128)}) while((s32[]{:T(128)}, f32[256,256]{0,1:T(8,128)S(1)}, s32[2,2]{1,0:T(2,128)S(1)}, f32[2,128,128]{2,1,0:T(8,128)S(1)}, s32[]{:T(128)}) %tuple.28), condition=%wide.while_cond, body=%wide.while_body.sunk | while | flops 2 | bytes 393321 | solution.py:78
  303.6 0.6 fusion.74
  304.2 1.4 dynamic-slice.7
  305.8 0.6 fusion.74
  306.4 1.4 dynamic-slice.7
  308.0 0.6 copy-done.10
  308.6 20.5 %custom-call.15 = f32[2,128,128]{1,2,0:T(8,128)S(1)} custom-call(f32[2,128,128]{2,1,0:T(8,128)} %copy-done.10), custom_call_target="InvertDiagBlocksLowerTriangular" | custom-call | tf_op jit(solution)/shard_map/triangular_solve | solution.py:78
  329.1 0.6 copy-done.2
  330.1 0.3 convolution_subtract_fusion.1
  330.4 1.2 fusion.27
  331.8 4.3 %gather_fusion.3 = f32[32,128,512]{2,1,0:T(8,128)} fusion(f32[2,4,128,512]{3,2,1,0:T(8,128)S(1)} %bitcast.80, s32[32]{0:T(128)S(1)} %reshape.277), kind=kCustom, calls=%fused_computation.3 | custom fusion | bytes 16777472 | tf_op jit(solution)/shard_map/jit(take_along_axis)/gather | solution.py:11
  336.1 0.4 fusion.21
  336.6 6.1 %select_reduce_fusion = f32[16,128,512]{2,1,0:T(8,128)S(1)} fusion(f32[2,16,128,512]{3,2,1,0:T(8,128)} %bitcast.82, pred[2,16]{1,0:T(4,128)(4,1)S(1)} %copy-done.9, pred[2,16]{1,0:T(4,128)(4,1)S(1)} %copy-done.8), kind=kLoop, calls=%fused_computation.10 | loop fusion | flops 5242880 | bytes 12582976 | tf_op jit(solution)/shard_map/reduce_sum | solution.py:92
  342.7 2.0 bitcast_select_fusion.1
  344.7 3.9 %fusion.12 = f32[2048,256]{1,0:T(8,128)} fusion(f32[2048,256]{1,0:T(8,128)S(1)} %get-tuple-element.45, f32[2048,256]{1,0:T(8,128)S(1)} %get-tuple-element.46, f32[256,256]{1,0:T(8,128)S(1)} %fusion.21, f32[2048,512]{1,0:T(8,128)S(1)} %bitcast.86, f32[256]{0:T(256)S(1)} %copy-done.6, s32[256]{0:T(256)S(1)} %copy-done.7, s32[2048]{0:T(1024)S(1)} %fusion.40, ...), kind=kOutput, calls=%fused_computation.18 | convolution fusion | flops 1613758464 | bytes 8663041 | tf_op jit(solution)/shard_map/dot_general | solution.py:107
  (74 shorter events, 3.2 us)
Async XLA Ops:
  6.5 79.4 %all-gather.2.cloned.1.call-start = ((), (), s32[]{:S(2)}) async-start(), calls=%async_computation.2 | async-start | bytes 17301504 | tf_op jit(solution)/shard_map/all_gather | solution.py:28
  7.3 255.2 %reduce-scatter.2.cloned.1.call-start = ((), (), s32[]{:S(2)}) async-start(), calls=%async_computation.3 | async-start | bytes 15728640 | tf_op jit(solution)/shard_map/reduce_scatter | solution.py:65
  110.3 1.9 copy-start.1
  148.8 0.7 copy-start.5
  148.8 6.9 %copy-start = (s32[2,16]{1,0:T(2,128)S(1)}, s32[2,16]{1,0:T(2,128)}, u32[]{:S(2)}) copy-start(s32[2,16]{1,0:T(2,128)} %param.4) | copy-start | bytes 388
  150.1 12.7 %all-to-all-start = ((f32[32,1,256]{2,1,0:T(1,128)}), f32[32,1,256]{2,1,0:T(1,128)S(1)}, u32[]{:S(2)}, u32[]{:S(2)}) async-start(f32[32,1,256]{2,1,0:T(1,128)} %stack.2), calls=%async_computation.1 | async-start | bytes 65536 | tf_op jit(solution)/shard_map/all_to_all | solution.py:32
  162.8 101.3 %copy-start.3 = (f32[1,1,256]{2,1,0:T(1,128)}, f32[1,1,256]{2,1,0:T(1,128)S(1)}, u32[]{:S(2)}) copy-start(f32[1,1,256]{2,1,0:T(1,128)S(1)} %slice.99) | copy-start | bytes 3076
  308.0 0.7 copy-start.10
  329.1 0.7 copy-start.2
  331.8 4.8 %copy-start.8 = (pred[2,16]{1,0:T(4,128)(4,1)S(1)}, pred[2,16]{1,0:T(4,128)(4,1)}, u32[]{:S(2)}) copy-start(pred[2,16]{1,0:T(4,128)(4,1)} %fusion.45) | copy-start | bytes 100
  331.8 4.8 %copy-start.9 = (pred[2,16]{1,0:T(4,128)(4,1)S(1)}, pred[2,16]{1,0:T(4,128)(4,1)}, u32[]{:S(2)}) copy-start(pred[2,16]{1,0:T(4,128)(4,1)} %compare_and_fusion) | copy-start | bytes 100
  336.6 6.1 %copy-start.4 = (f32[1,1,256]{2,1,0:T(1,128)S(1)}, f32[1,1,256]{2,1,0:T(1,128)}, u32[]{:S(2)}) copy-start(f32[1,1,256]{2,1,0:T(1,128)} %copy-done.3) | copy-start | bytes 3076
  342.7 2.1 copy-start.6
  342.7 2.1 copy-start.7
Sparse Core Ops, SparseCore 0:
  9.6 76.2 all-gather.1
  149.0 113.4 reduce-scatter.1
